TPU v7x, 32 devices: a whole 2x2x4 slice. The times are simulated.
32 devices in a mesh: groups: 2 (over y), expert: 4 (over z), dp: 4 (over x, core).
Axes of the slice: x: 2, y: 2, z: 4, core: 2. Of those that a mesh axis runs over, the one named last changes fastest.
Arguments:
- out_grad: bfloat16 [4096, 2048], P(('groups', 'expert', 'dp')), parts along dimension 0, may hold values from -0.5 to 0.5
- gate_weights: bfloat16 [4096, 8], P(('groups', 'expert', 'dp')), parts along dimension 0, may hold values from 0.049804688 to 0.5
- expert_ids: int32 [4096, 8], P(('groups', 'expert', 'dp')), parts along dimension 0, may hold values from 0 to 31, all different within a row; in each aligned block of 128 rows (0 to 127, 128 to 255, ...) at most 36 rows name the same one
- hidden: bfloat16 [32, 8, 4, 36, 768], P('expert', ('groups', 'dp')), parts along dimension 1, may hold values from -6 to 6
- down_weight: bfloat16 [32, 768, 2048], P('expert', None, 'dp'), may hold values from -0.21875 to 0.21875
Outputs:
- weight_grad: float32 [64, 768, 2048], P(('groups', 'expert'), None, 'dp'), parts along dimension 0
- gate_grad: float32 [4096, 8], P(('groups', 'expert', 'dp')), parts along dimension 0
There are 2 independent parts, one for each index of `groups`. A program takes and returns all parts, laid end to end along the dimension named above; an argument that names none is the same for every part. Nothing has to cross between parts.
Inputs may be any that keep to these rules, and one draw needn't show every extreme that they name: `expert_ids`: each token names 8 different experts; within each block of 128 tokens (one device's tokens) no expert is named by more than 36 tokens, a bound that some block reaches.
All inputs are finite; a program needn't handle non-finite values.
Results may differ from a plain program's by a relative error of at most 0.0095.
Values may be sent and summed in bfloat16 or wider, within the bound.
No kernel may reach another device: no remote copies, remote signals or barrier semaphores. Data moves between devices by JAX's collectives and lax.ppermute only.
A program may use at most 128 MiB of HBM per device.

v0:
```python
import jax
import jax.numpy as jnp
from jax import lax
from jax.sharding import PartitionSpec as P


def per_device(out_grad, gate_weights, expert_ids, hidden, down_weight):
    tok_rows, top_count = expert_ids.shape
    row_width = out_grad.shape[1]
    local_count = hidden.shape[0]
    capacity = hidden.shape[3]
    peer_count = lax.axis_size("expert")
    shards = lax.axis_size("dp")
    expert_count = local_count * peer_count
    col_width = row_width // shards
    block_count = peer_count * shards
    f32 = jnp.float32
    bf16 = jnp.bfloat16
    my_dp = lax.axis_index("dp")
    fetched = lax.ppermute(hidden, "dp", [(j, j ^ 2) for j in range(shards)])
    paired = lax.ppermute(
        jnp.concatenate([hidden, fetched], axis=1), "dp", [(j, j ^ 1) for j in range(shards)]
    )
    pieces = [hidden, fetched, paired[:, 0:1], paired[:, 1:2]]
    piece_replica = [my_dp, my_dp ^ 2, my_dp ^ 1, my_dp ^ 3]
    meta = jnp.concatenate([expert_ids.astype(bf16), gate_weights], axis=1).reshape(-1)
    meta_len = meta.shape[0]
    meta_rows = -(-meta_len // col_width)
    meta = jnp.pad(meta, (0, meta_rows * col_width - meta_len)).reshape(meta_rows, 1, col_width)
    cols = out_grad.reshape(tok_rows, shards, col_width)
    cols = jnp.concatenate([cols, jnp.broadcast_to(meta, (meta_rows, shards, col_width))], axis=0)
    cols = lax.all_to_all(cols, "dp", split_axis=1, concat_axis=0, tiled=True)
    cols = cols.reshape(shards, tok_rows + meta_rows, col_width)
    got = lax.all_gather(cols, "expert", axis=0, tiled=False)
    got = got.reshape(block_count, tok_rows + meta_rows, col_width)
    grad_all = got[:, :tok_rows]
    meta_all = got[:, tok_rows:].reshape(block_count, meta_rows * col_width)[:, :meta_len]
    meta_all = meta_all.reshape(block_count, tok_rows, 2 * top_count)
    ids_all = meta_all[:, :, :top_count].astype(jnp.int32)
    gate_all = meta_all[:, :, top_count:]
    my_experts = lax.axis_index("expert") * local_count + jnp.arange(local_count, dtype=jnp.int32)
    hit = ids_all[:, :, :, None] == my_experts[None, None, None, :]
    chose = jnp.any(hit, axis=2)
    gate_hit = jnp.sum(jnp.where(hit, gate_all.astype(f32)[:, :, :, None], 0.0), axis=2)
    before = (jnp.arange(tok_rows)[:, None] < jnp.arange(tok_rows)[None, :]).astype(bf16)
    rank = jnp.einsum("bul,ut->btl", chose.astype(bf16), before, preferred_element_type=f32).astype(
        jnp.int32
    )
    slot_ids = jnp.arange(capacity, dtype=jnp.int32)
    chose_t = chose.transpose(0, 2, 1)
    rank_t = rank.transpose(0, 2, 1)
    gate_t = gate_hit.transpose(0, 2, 1)
    select = chose_t[:, :, None, :] & (rank_t[:, :, None, :] == slot_ids[None, None, :, None])
    select_gate = jnp.where(select, gate_t[:, :, None, :], 0.0).astype(bf16)
    grad_rows = jnp.einsum(
        "blct,btd->blcd", select.astype(bf16), grad_all, preferred_element_type=f32
    ).astype(bf16)
    scaled = jnp.einsum("blct,btd->blcd", select_gate, grad_all, preferred_element_type=f32).astype(
        bf16
    )
    grad_rows = grad_rows.reshape(peer_count, shards, local_count, capacity, col_width)
    scaled = scaled.reshape(peer_count, shards, local_count, capacity, col_width)
    weight_grad = None
    slot_part = jnp.zeros((peer_count, shards, local_count, capacity), f32)
    for piece, replica in zip(pieces, piece_replica):
        piece = piece[:, 0]
        scaled_r = lax.dynamic_index_in_dim(scaled, replica, axis=1, keepdims=False)
        rows_r = lax.dynamic_index_in_dim(grad_rows, replica, axis=1, keepdims=False)
        part = (
            jnp.einsum("lscf,slcd->lfd", piece, scaled_r, preferred_element_type=f32)
            .astype(bf16)
            .astype(f32)
        )
        weight_grad = part if weight_grad is None else weight_grad + part
        expert_out = jnp.einsum("lscf,lfd->slcd", piece, down_weight, preferred_element_type=f32)
        slot_r = jnp.sum(rows_r.astype(f32) * expert_out, axis=3)
        slot_part = lax.dynamic_update_index_in_dim(slot_part, slot_r, replica, axis=1)
    send_back = slot_part.reshape(block_count, local_count, capacity)
    returned = lax.all_to_all(send_back, ("expert", "dp"), split_axis=0, concat_axis=0, tiled=True)
    returned = returned.reshape(peer_count, shards, local_count, capacity)
    slot_grad = jnp.sum(returned, axis=1).reshape(expert_count, capacity)
    own_hit = expert_ids[:, :, None] == jnp.arange(expert_count, dtype=jnp.int32)[None, None, :]
    own_chose = jnp.any(own_hit, axis=1)
    own_rank = jnp.einsum(
        "ue,ut->te", own_chose.astype(bf16), before, preferred_element_type=f32
    ).astype(jnp.int32)
    own_slot = jnp.sum(jnp.where(own_hit, own_rank[:, None, :], 0), axis=2)
    by_slot = jnp.sum(jnp.where(own_hit[:, :, :, None], slot_grad[None, None], 0.0), axis=2)
    gate_grad = jnp.sum(
        jnp.where(own_slot[:, :, None] == slot_ids[None, None, :], by_slot, 0.0), axis=2
    )
    return (weight_grad, gate_grad)


def solution(mesh):
    return jax.shard_map(
        per_device,
        mesh=mesh,
        in_specs=(
            P(("groups", "expert", "dp"), None),
            P(("groups", "expert", "dp"), None),
            P(("groups", "expert", "dp"), None),
            P("expert", ("groups", "dp"), None, None, None),
            P("expert", None, "dp"),
        ),
        out_specs=(P(("groups", "expert"), None, "dp"), P(("groups", "expert", "dp"), None)),
        check_vma=False,
    )
```

profile of v0, /device:TPU:0, one launch (start us, length us, event | category | flops | bytes accessed | tf_op | source)
XLA Modules:
  0.0 151.6 jit_solution(17778870522974405558)
XLA Ops:
  7.2 0.0 all-gather.3.cloned.1.call-start
  7.2 0.7 convert_element_type.81
  7.9 0.7 pad_maximum_fusion.2
  8.6 0.1 copy.187
  8.7 0.1 broadcast_in_dim.100
  8.8 0.2 copy.188
  9.0 1.3 copy.186
  10.3 0.1 broadcast_in_dim.101
  10.4 0.2 pad_maximum_fusion.1
  10.6 0.5 copy.189
  11.1 13.3 %all_to_all.20 = bf16[132,4,512]{2,0,1:T(8,128)(2,1)} all-to-all(bf16[132,4,512]{2,0,1:T(8,128)(2,1)S(1)} %copy.189), channel_id=1, replica_groups=mesh['groups'=2,'expert'=4,'dp'=4] {'dp'}, dimensions={1} | all-to-all | bytes 1081344 | tf_op jit(solution)/shard_map/all_to_all | solution.py:32
  24.4 0.0 all-gather.3.cloned.1.call-update
  24.4 2.0 %copy.196 = bf16[8,1,4,36,768]{4,0,3,2,1:T(8,128)(2,1)S(1)} copy(bf16[8,1,4,36,768]{4,2,3,1,0:T(4,128)(2,1)} %param.8) | data formatting | bytes 3538944 | tf_op args[3]
  26.4 0.4 collective-permute-start
  26.9 0.6 fusion.51
  27.5 0.1 convolution_convert_fusion.3
  27.7 39.3 %collective-permute-done = bf16[8,1,4,36,768]{4,0,3,2,1:T(8,128)(2,1)S(1)} collective-permute-done((bf16[8,1,4,36,768]{4,0,3,2,1:T(8,128)(2,1)S(1)}, bf16[8,1,4,36,768]{4,0,3,2,1:T(8,128)(2,1)S(1)}, u32[]{:S(2)}, u32[]{:S(2)}) %collective-permute-start) | collective-permute-done | bytes 1769504 | tf_op jit(solution)/shard_map/ppermute | solution.py:20
  67.0 2.3 %pad_maximum_fusion = bf16[8,2,4,36,768]{4,0,3,2,1:T(8,128)(2,1)} fusion(bf16[8,1,4,36,768]{4,0,3,2,1:T(8,128)(2,1)S(1)} %collective-permute-done, bf16[8,1,4,36,768]{4,0,3,2,1:T(8,128)(2,1)S(1)} %copy.196), kind=kLoop, calls=%fused_computation.15 | loop fusion | flops 1769472 | bytes 7077888 | tf_op jit(solution)/shard_map/concatenate | solution.py:22
  69.3 0.1 copy-done.3
  69.3 0.0 collective-permute-start.1
  69.3 4.3 %all-gather.3.cloned.1.call-done = bf16[16,132,1,512]{3,1,2,0:T(8,128)(2,1)} async-done(((bf16[4,132,1,512]{3,1,2,0:T(8,128)(2,1)}), bf16[16,132,1,512]{3,1,2,0:T(8,128)(2,1)}) %all-gather.3.cloned.1.call-update) | async-done | bytes 2162704 | tf_op jit(solution)/shard_map/all_gather | solution.py:34
  73.7 0.9 slice.24
  74.6 0.4 reshape_reshape.3
  75.0 1.0 fusion.56
  76.0 1.2 copy.226
  77.2 0.2 copy.233
  77.4 0.1 compare_reduce_fusion
  77.6 0.1 fusion.50
  77.7 0.1 convolution_convert_fusion.2
  77.9 1.5 convolution_convert_fusion.1
  79.4 0.1 copy-done.2
  79.5 1.5 %convolution_convert_fusion = bf16[16,8,36,512]{3,2,1,0:T(8,128)(2,1)S(1)} fusion(bf16[16,132,512]{2,1,0:T(8,128)(2,1)S(1)} %bitcast.135, bf16[16,8,128]{2,1,0:T(8,128)(2,1)S(1)} %bitcast.142, s32[16,8,128]{2,1,0:T(8,128)S(1)} %convolution_convert_fusion.2, pred[16,8,128]{2,1,0:T(8,128)(4,1)S(1)} %bitcast.141), kind=kOutput, calls=%fused_computation.16 | convolution fusion | flops 608108544 | bytes 6930432 | tf_op jit(solution)/shard_map/blct,btd->blcd/dot_general | solution.py:58
  81.0 4.1 %constant_dynamic-slice_fusion = (bf16[4,1,8,36,512]{4,3,2,1,0:T(8,128)(2,1)}, bf16[4,1,8,36,512]{4,3,2,1,0:T(8,128)(2,1)}, bf16[4,1,8,36,512]{4,3,2,1,0:T(8,128...) fusion(bf16[4,4,8,36,512]{4,3,2,1,0:T(8,128)(2,1)S(1)} %bitcast, ...), kind=kLoop, calls=%fused_computation.78 | loop fusion | bytes 18874384 | tf_op jit(solution)/shard_map/jit(dynamic_index_in_dim)/dynamic_slice | solution.py:68
  85.1 5.0 %fusion.12 = f32[4,8,36]{2,0,1:T(4,128)S(1)} fusion(bf16[4,1,8,36,512]{4,3,2,1,0:T(8,128)(2,1)} %get-tuple-element.21, bf16[8,4,36,768]{3,1,2,0:T(4,128)(2,1)} %bitcast.138, bf16[8,768,512]{2,1,0:T(8,128)(2,1)} %param.9), kind=kOutput, calls=%fused_computation.25 | convolution fusion | flops 907737984 | bytes 9245184 | tf_op jit(solution)/shard_map/lscf,lfd->slcd/dot_general | solution.py:75
  90.2 0.6 broadcast_in_dim.109
  90.8 0.6 copy_dynamic-update-slice_fusion.3
  91.4 0.0 copy-done.4
  91.4 0.0 slice-start
  91.4 4.3 %fusion.11 = f32[4,8,36]{2,0,1:T(4,128)S(1)} fusion(bf16[4,1,8,36,512]{4,3,2,1,0:T(8,128)(2,1)S(1)} %copy-done.10, bf16[8,1,4,36,768]{4,0,3,2,1:T(8,128)(2,1)S(1)} %copy-done.4, bf16[8,768,512]{2,1,0:T(8,128)(2,1)} %param.9), kind=kOutput, calls=%fused_computation.23 | convolution fusion | flops 907737984 | bytes 9245184 | tf_op jit(solution)/shard_map/lscf,lfd->slcd/dot_general | solution.py:75
  95.7 0.6 copy_dynamic-update-slice_fusion.2
  96.4 4.6 %fusion.22 = bf16[8,512,768,1]{2,1,3,0:T(8,128)(2,1)} fusion(bf16[8,4,36,768]{3,1,2,0:T(4,128)(2,1)S(1)} %bitcast.139, bf16[4,1,8,36,512]{4,3,2,1,0:T(8,128)(2,1)S(1)} %copy-done.9), kind=kOutput, calls=%fused_computation.39 | convolution fusion | flops 905969664 | bytes 9240576 | tf_op jit(solution)/shard_map/lscf,slcd->lfd/dot_general | solution.py:70
  101.0 0.0 collective-permute-done.1
  101.0 2.3 %fusion.55 = (bf16[8,1,4,36,768]{4,0,3,2,1:T(8,128)(2,1)S(1)}, bf16[8,1,4,36,768]{4,0,3,2,1:T(8,128)(2,1)S(1)}) fusion(bf16[8,2,4,36,768]{4,0,3,2,1:T(8,128)(2,1)} %collective-permute-done.1), kind=kLoop, calls=%fused_computation.88 | loop fusion | bytes 7077888 | tf_op jit(solution)/shard_map/slice | solution.py:24
  103.4 0.0 slice-done
  103.4 0.0 slice-done.1
  103.4 0.0 copy-done.8
  103.4 1.6 %fusion.9 = f32[4,8,36]{2,0,1:T(4,128)S(1)} fusion(bf16[4,1,8,36,512]{4,3,2,1,0:T(8,128)(2,1)S(1)} %copy-done.8, bf16[8,768,512]{2,1,0:T(8,128)(2,1)S(1)} %bitcast.149, bf16[8,1,4,36,768]{4,0,3,2,1:T(8,128)(2,1)S(1)} %get-tuple-element.26), kind=kOutput, calls=%fused_computation.19 | convolution fusion | flops 907737984 | bytes 9245184 | tf_op jit(solution)/shard_map/lscf,lfd->slcd/dot_general | solution.py:75
  105.0 1.8 %fusion.10 = f32[4,8,36]{2,0,1:T(4,128)S(1)} fusion(bf16[4,1,8,36,512]{4,3,2,1,0:T(8,128)(2,1)S(1)} %copy-done.7, bf16[8,768,512]{2,1,0:T(8,128)(2,1)S(1)} %bitcast.149, bf16[8,1,4,36,768]{4,0,3,2,1:T(8,128)(2,1)S(1)} %get-tuple-element.27), kind=kOutput, calls=%fused_computation.21 | convolution fusion | flops 907737984 | bytes 9245184 | tf_op jit(solution)/shard_map/lscf,lfd->slcd/dot_general | solution.py:75
  106.8 0.6 copy_dynamic-update-slice_fusion.1
  107.4 0.6 copy_dynamic-update-slice_fusion
  108.0 1.6 %reshape.70 = f32[16,1,288]{2,1,0:T(1,128)} reshape(f32[16,8,36]{2,1,0:T(8,128)} %bitcast.43) | data formatting | bytes 36864
  109.5 4.1 %all-to-all-start.1 = ((f32[16,1,288]{2,1,0:T(1,128)}), f32[16,1,288]{2,1,0:T(1,128)}, u32[]{:S(2)}, u32[]{:S(2)}) async-start(f32[16,1,288]{2,1,0:T(1,128)} %reshape.70), calls=%async_computation.1 | async-start | bytes 49152 | tf_op jit(solution)/shard_map/all_to_all | solution.py:79
  113.7 3.4 %fusion.17 = bf16[8,768,512,1]{1,2,3,0:T(8,128)(2,1)S(1)} fusion(bf16[8,1,4,36,768]{4,0,3,2,1:T(8,128)(2,1)S(1)} %get-tuple-element.27, bf16[4,1,8,36,512]{4,3,2,1,0:T(8,128)(2,1)} %get-tuple-element.33), kind=kOutput, calls=%fused_computation.34 | convolution fusion | flops 905969664 | bytes 9240576 | tf_op jit(solution)/shard_map/lscf,slcd->lfd/dot_general | solution.py:70
  117.0 0.0 copy-done
  117.1 1.9 %fusion.18 = bf16[8,768,512,1]{1,2,3,0:T(8,128)(2,1)S(1)} fusion(bf16[8,1,4,36,768]{4,0,3,2,1:T(8,128)(2,1)S(1)} %get-tuple-element.26, bf16[4,1,8,36,512]{4,3,2,1,0:T(8,128)(2,1)S(1)} %copy-done), kind=kOutput, calls=%fused_computation.35 | convolution fusion | flops 905969664 | bytes 9240576 | tf_op jit(solution)/shard_map/lscf,slcd->lfd/dot_general | solution.py:70
  119.0 9.5 %fusion = f32[8,768,512]{1,2,0:T(8,128)} fusion(bf16[8,512,768,1]{2,1,3,0:T(8,128)(2,1)} %fusion.22, bf16[8,768,512,1]{1,2,3,0:T(8,128)(2,1)S(1)} %fusion.17, bf16[8,768,512,1]{1,2,3,0:T(8,128)(2,1)S(1)} %fusion.18, bf16[8,1,4,36,768]{4,0,3,2,1:T(8,128)(2,1)S(1)} %copy-done.5, bf16[4,1,8,36,512]{4,3,2,1,0:T(8,128)(2,1)} %get-tuple-element.35), kind=kOutput, calls=%fused_computation.3 | convolution fusion | flops 931135488 | bytes 34406400 | tf_op jit(solution)/shard_map/lscf,slcd->lfd/dot_general | solution.py:70
  128.5 12.6 %copy.216 = f32[8,768,512]{2,1,0:T(8,128)} copy(f32[8,768,512]{1,2,0:T(8,128)} %fusion) | data formatting | bytes 25165824
  141.1 0.0 all-to-all-done.1
  141.1 0.5 broadcast.17
  141.6 1.4 reduce
  143.1 0.1 reshape.71
  143.2 0.1 copy.214
  143.3 0.8 select_reduce_fusion
  144.1 0.6 select_reduce_fusion.1
  (28 shorter events, 0.1 us)
Async XLA Ops:
  7.2 66.5 %all-gather.3.cloned.1.call-start = ((), (), s32[]{:S(2)}) async-start(), calls=%async_computation.2 | async-start | bytes 2785280 | tf_op jit(solution)/shard_map/all_gather | solution.py:34
  24.4 2.5 %copy-start.12 = (s32[128,8]{0,1:T(8,128)S(1)}, s32[128,8]{0,1:T(8,128)}, u32[]{:S(2)}) copy-start(s32[128,8]{0,1:T(8,128)} %param.7) | copy-start | bytes 12292
  26.4 40.5 %collective-permute-start = (bf16[8,1,4,36,768]{4,0,3,2,1:T(8,128)(2,1)S(1)}, bf16[8,1,4,36,768]{4,0,3,2,1:T(8,128)(2,1)S(1)}, u32[]{:S(2)}, u32[]{:S(2)}) collective-permute-start(bf16[8,1,4,36,768]{4,0,3,2,1:T(8,128)(2,1)S(1)} %copy.196), channel_id=1, source_target_pairs={{0,2},{1,3},{2,0},{3,1},{4,6},{5,7},{6,4},{7,5},{8,10},{9,11},{10,... | collective-permute-start | bytes 5308424 | tf_op jit(solution)/shard_map/ppermute | solution.py:20
  67.0 2.4 %copy-start.3 = (bf16[8,1,4,36,768]{4,0,3,2,1:T(8,128)(2,1)}, bf16[8,1,4,36,768]{4,0,3,2,1:T(8,128)(2,1)S(1)}, u32[]{:S(2)}) copy-start(bf16[8,1,4,36,768]{4,0,3,2,1:T(8,128)(2,1)S(1)} %collective-permute-done) | copy-start | bytes 5308420
  69.3 31.7 %collective-permute-start.1 = (bf16[8,2,4,36,768]{4,0,3,2,1:T(8,128)(2,1)}, bf16[8,2,4,36,768]{4,0,3,2,1:T(8,128)(2,1)}, u32[]{:S(2)}, u32[]{:S(2)}) collective-permute-start(bf16[8,2,4,36,768]{4,0,3,2,1:T(8,128)(2,1)} %pad_maximum_fusion), channel_id=1, source_target_pairs={{0,1},{1,0},{2,3},{3,2},{4,5},{5,4},{6,7},{7,6},{8,9},{9,8},{10,11... | collective-permute-start | bytes 10616840 | tf_op jit(solution)/shard_map/ppermute | solution.py:21
  75.0 2.9 %copy-start.1 = (bf16[16,132,1,512]{3,1,2,0:T(8,128)(2,1)S(1)}, bf16[16,132,1,512]{3,1,2,0:T(8,128)(2,1)}, u32[]{:S(2)}) copy-start(bf16[16,132,1,512]{3,1,2,0:T(8,128)(2,1)} %all-gather.3.cloned.1.call-done) | copy-start | bytes 6488068
  77.9 1.6 %copy-start.2 = (bf16[16,132,1,512]{3,1,2,0:T(8,128)(2,1)S(1)}, bf16[16,132,1,512]{3,1,2,0:T(8,128)(2,1)}, u32[]{:S(2)}) copy-start(bf16[16,132,1,512]{3,1,2,0:T(8,128)(2,1)} %all-gather.3.cloned.1.call-done) | copy-start | bytes 6488068
  85.1 6.3 %copy-start.4 = (bf16[8,1,4,36,768]{4,0,3,2,1:T(8,128)(2,1)S(1)}, bf16[8,1,4,36,768]{4,0,3,2,1:T(8,128)(2,1)}, u32[]{:S(2)}) copy-start(bf16[8,1,4,36,768]{4,0,3,2,1:T(8,128)(2,1)} %copy-done.3) | copy-start | bytes 5308420
  85.1 6.3 %copy-start.10 = (bf16[4,1,8,36,512]{4,3,2,1,0:T(8,128)(2,1)S(1)}, bf16[4,1,8,36,512]{4,3,2,1,0:T(8,128)(2,1)}, u32[]{:S(2)}) copy-start(bf16[4,1,8,36,512]{4,3,2,1,0:T(8,128)(2,1)} %get-tuple-element.20) | copy-start | bytes 3538948
  91.4 5.0 %copy-start.6 = (bf16[8,1,4,36,768]{4,2,3,1,0:T(4,128)(2,1)S(1)}, bf16[8,1,4,36,768]{4,2,3,1,0:T(4,128)(2,1)}, u32[]{:S(2)}) copy-start(bf16[8,1,4,36,768]{4,2,3,1,0:T(4,128)(2,1)} %param.8) | copy-start | bytes 5308420
  91.4 5.0 %copy-start.9 = (bf16[4,1,8,36,512]{4,3,2,1,0:T(8,128)(2,1)S(1)}, bf16[4,1,8,36,512]{4,3,2,1,0:T(8,128)(2,1)}, u32[]{:S(2)}) copy-start(bf16[4,1,8,36,512]{4,3,2,1,0:T(8,128)(2,1)} %get-tuple-element.32) | copy-start | bytes 3538948
  91.4 12.0 %slice-start = ((s8[6291456]{0:T(1024)(128)(4,1)}), s8[2097152]{0:T(1024)(128)(4,1)S(1)}, s32[]{:S(2)}) async-start(s8[6291456]{0:T(1024)(128)(4,1)} %bitcast.148), calls=%async_computation.3 | async-start | bytes 4194304
  96.4 7.0 %slice-start.1 = ((s8[6291456]{0:T(1024)(128)(4,1)}), s8[4194304]{0:T(1024)(128)(4,1)S(1)}, s32[]{:S(2)}) async-start(s8[6291456]{0:T(1024)(128)(4,1)} %bitcast.148), calls=%async_computation.4 | async-start | bytes 8388608
  101.0 2.4 %copy-start.8 = (bf16[4,1,8,36,512]{4,3,2,1,0:T(8,128)(2,1)S(1)}, bf16[4,1,8,36,512]{4,3,2,1,0:T(8,128)(2,1)}, u32[]{:S(2)}) copy-start(bf16[4,1,8,36,512]{4,3,2,1,0:T(8,128)(2,1)} %get-tuple-element.18) | copy-start | bytes 3538948
  103.4 1.6 %copy-start.7 = (bf16[4,1,8,36,512]{4,3,2,1,0:T(8,128)(2,1)S(1)}, bf16[4,1,8,36,512]{4,3,2,1,0:T(8,128)(2,1)}, u32[]{:S(2)}) copy-start(bf16[4,1,8,36,512]{4,3,2,1,0:T(8,128)(2,1)} %get-tuple-element.19) | copy-start | bytes 3538948
  109.5 31.6 %all-to-all-start.1 = ((f32[16,1,288]{2,1,0:T(1,128)}), f32[16,1,288]{2,1,0:T(1,128)}, u32[]{:S(2)}, u32[]{:S(2)}) async-start(f32[16,1,288]{2,1,0:T(1,128)} %reshape.70), calls=%async_computation.1 | async-start | bytes 49152 | tf_op jit(solution)/shard_map/all_to_all | solution.py:79
  113.7 3.4 %copy-start = (bf16[4,1,8,36,512]{4,3,2,1,0:T(8,128)(2,1)S(1)}, bf16[4,1,8,36,512]{4,3,2,1,0:T(8,128)(2,1)}, u32[]{:S(2)}) copy-start(bf16[4,1,8,36,512]{4,3,2,1,0:T(8,128)(2,1)} %get-tuple-element.34) | copy-start | bytes 3538948
  117.1 2.0 %copy-start.5 = (bf16[8,1,4,36,768]{4,0,3,2,1:T(8,128)(2,1)S(1)}, bf16[8,1,4,36,768]{4,0,3,2,1:T(8,128)(2,1)}, u32[]{:S(2)}) copy-start(bf16[8,1,4,36,768]{4,0,3,2,1:T(8,128)(2,1)} %copy-done.3) | copy-start | bytes 5308420
  128.5 14.8 %copy-start.11 = (pred[128,8,32]{0,2,1:T(8,128)(4,1)S(1)}, pred[128,8,32]{0,2,1:T(8,128)(4,1)}, u32[]{:S(2)}) copy-start(pred[128,8,32]{0,2,1:T(8,128)(4,1)} %get-tuple-element.31) | copy-start | bytes 98308
Sparse Core Ops, SparseCore 0:
  24.6 49.0 all-gather.2
where the time goes:
time: 152 us
  waiting for transfers between devices  43.6 us (29%)
  matrix products  35.5 us (23%)
  local copies, waits for them, and re-layouts  32.5 us (21%)
  between operations  14.3 us (9%)
  blocking collectives  13.3 us (9%)
  other arithmetic  7.75 us (5%)
  starting transfers between devices  4.59 us (3%)
    ppermute x1, waiting for transfers between devices, per_device(): fetched = lax.ppermute(hidden, 'dp', [(j, j ^ 2) for j in range(shards)])  39.3 us
    dot_general x4, matrix products, per_device(): jnp.einsum('lscf,slcd->lfd', piece, scaled_r, preferred_element_type=f32)  19.4 us
    unnamed x37, local copies, waits for them, and re-layouts  19.2 us
    all_to_all x1, blocking collectives, per_device(): cols = lax.all_to_all(cols, 'dp', split_axis=1, concat_axis=0, tiled=True)  13.3 us
    dot_general x4, matrix products, per_device(): jnp.einsum('lscf,lfd->slcd', piece, down_weight, preferred_element_type=f32)  12.7 us
    all_gather x1, waiting for transfers between devices, per_device(): got = lax.all_gather(cols, 'expert', axis=0, tiled=False)  4.34 us
    all_to_all x1, starting transfers between devices, per_device(): lax.all_to_all(send_back, ('expert', 'dp'), split_axis=0, concat_axis=0,...  4.13 us
    dynamic_slice x1, local copies, waits for them, and re-layouts, per_device(): lax.dynamic_index_in_dim(grad_rows, replica, axis=1, keepdims=False)  4.08 us
  transfers between devices with their start and end apart: 4, of which 2 were waited for; matrix products, arithmetic and copies ran while one was open for 39% of the time, Pallas kernels for 0%

commit v1 on v0

--- a/solution.py
+++ b/solution.py
@@ -29,7 +29,9 @@
     meta = jnp.pad(meta, (0, meta_rows * col_width - meta_len)).reshape(meta_rows, 1, col_width)
     cols = out_grad.reshape(tok_rows, shards, col_width)
     cols = jnp.concatenate([cols, jnp.broadcast_to(meta, (meta_rows, shards, col_width))], axis=0)
-    cols = lax.all_to_all(cols, "dp", split_axis=1, concat_axis=0, tiled=True)
+    cols = jnp.concatenate(
+        lax.all_to_all(jnp.stack(jnp.split(cols, lax.axis_size("dp"), axis=1)), "dp", 0, 0), axis=0
+    )
     cols = cols.reshape(shards, tok_rows + meta_rows, col_width)
     got = lax.all_gather(cols, "expert", axis=0, tiled=False)
     got = got.reshape(block_count, tok_rows + meta_rows, col_width)

time: 152 us -> 153 us (level)
    unnamed x37 -> x39, local copies, waits for them, and re-layouts: 19.2 us -> 17.7 us
  transfers between devices with their start and end apart: 4 -> 4, of which waited for: 2 -> 2; matrix products, arithmetic and copies ran while one was open for 39% -> 38% of each run, Pallas kernels for 0% -> 0%
where the time goes in v1:
time: 153 us; the launch traced here: 152 us
  waiting for transfers between devices  45.1 us (29%)
  matrix products  35.4 us (23%)
  local copies, waits for them, and re-layouts  31 us (20%)
  between operations  14.3 us (9%)
  blocking collectives  13.4 us (9%)
  other arithmetic  7.99 us (5%)
  starting transfers between devices  4.59 us (3%)
    ppermute x1, waiting for transfers between devices, per_device(): fetched = lax.ppermute(hidden, 'dp', [(j, j ^ 2) for j in range(shards)])  39.3 us
    dot_general x4, matrix products, per_device(): jnp.einsum('lscf,slcd->lfd', piece, scaled_r, preferred_element_type=f32)  19.4 us
    unnamed x39, local copies, waits for them, and re-layouts  17.7 us
    all_to_all x1, blocking collectives, per_device(): lax.all_to_all(jnp.stack(jnp.split(cols, lax.axis_size('dp'), axis=1)), '...  13.4 us
    dot_general x4, matrix products, per_device(): jnp.einsum('lscf,lfd->slcd', piece, down_weight, preferred_element_type=f32)  12.7 us
    all_gather x1, waiting for transfers between devices, per_device(): got = lax.all_gather(cols, 'expert', axis=0, tiled=False)  5.8 us
    all_to_all x1, starting transfers between devices, per_device(): lax.all_to_all(send_back, ('expert', 'dp'), split_axis=0, concat_axis=0,...  4.13 us
    dynamic_slice x1, local copies, waits for them, and re-layouts, per_device(): lax.dynamic_index_in_dim(grad_rows, replica, axis=1, keepdims=False)  4.08 us
  transfers between devices with their start and end apart: 4, of which 2 were waited for; matrix products, arithmetic and copies ran while one was open for 38% of the time, Pallas kernels for 0%

profile of v1, /device:TPU:0, one launch (start us, length us, event | category | flops | bytes accessed | tf_op | source)
XLA Modules:
  0.0 151.9 jit_solution(13288997874657462983)
XLA Ops:
  7.2 0.0 all-gather.3.cloned.1.call-start
  7.2 0.7 convert_element_type.81
  7.9 0.7 pad_maximum_fusion.3
  8.6 0.1 copy.162
  8.7 0.1 broadcast_in_dim.100
  8.8 0.2 copy.163
  9.0 1.3 copy.161
  10.3 0.1 broadcast_in_dim.101
  10.4 0.2 fusion.55
  10.6 0.2 pad_maximum_fusion.1
  10.9 0.0 copy-start.6
  10.9 0.5 copy.164
  11.4 13.4 %all_to_all.10 = bf16[4,132,1,512]{3,1,2,0:T(8,128)(2,1)} all-to-all(bf16[4,132,1,512]{3,1,2,0:T(8,128)(2,1)S(1)} %copy.164), channel_id=1, replica_groups=mesh['groups'=2,'expert'=4,'dp'=4] {'dp'}, dimensions={0} | all-to-all | bytes 1081344 | tf_op jit(solution)/shard_map/all_to_all | solution.py:33
  24.8 0.0 all-gather.3.cloned.1.call-update
  24.8 0.5 copy.170
  25.4 0.4 collective-permute-start
  25.8 0.6 fusion.58
  26.4 0.1 convolution_convert_fusion.3
  26.6 39.3 %collective-permute-done = bf16[8,1,4,36,768]{4,0,3,2,1:T(8,128)(2,1)S(1)} collective-permute-done((bf16[8,1,4,36,768]{4,0,3,2,1:T(8,128)(2,1)S(1)}, bf16[8,1,4,36,768]{4,0,3,2,1:T(8,128)(2,1)S(1)}, u32[]{:S(2)}, u32[]{:S(2)}) %collective-permute-start) | collective-permute-done | bytes 1769504 | tf_op jit(solution)/shard_map/ppermute | solution.py:20
  65.9 2.3 %pad_maximum_fusion = bf16[8,2,4,36,768]{4,0,3,2,1:T(8,128)(2,1)} fusion(bf16[8,1,4,36,768]{4,0,3,2,1:T(8,128)(2,1)S(1)} %collective-permute-done, bf16[8,1,4,36,768]{4,0,3,2,1:T(8,128)(2,1)S(1)} %copy.170), kind=kLoop, calls=%fused_computation.15 | loop fusion | flops 1769472 | bytes 7077888 | tf_op jit(solution)/shard_map/concatenate | solution.py:22
  68.2 0.1 copy-done.3
  68.3 0.0 collective-permute-start.1
  68.3 5.8 %all-gather.3.cloned.1.call-done = bf16[16,132,1,512]{3,1,2,0:T(8,128)(2,1)} async-done(((bf16[4,132,1,512]{3,1,2,0:T(8,128)(2,1)}), bf16[16,132,1,512]{3,1,2,0:T(8,128)(2,1)}) %all-gather.3.cloned.1.call-update) | async-done | bytes 2162704 | tf_op jit(solution)/shard_map/all_gather | solution.py:36
  74.1 0.9 slice.24
  75.0 0.4 reshape_reshape.3
  75.4 1.0 fusion.63
  76.4 1.2 copy.200
  77.6 0.2 copy.207
  77.8 0.1 compare_reduce_fusion
  78.0 0.1 fusion.50
  78.1 0.1 convolution_convert_fusion.2
  78.2 0.0 copy-done.1
  78.2 0.0 copy-start.2
  78.3 1.5 convolution_convert_fusion.1
  79.8 0.1 copy-done.2
  79.9 1.5 %convolution_convert_fusion = bf16[16,8,36,512]{3,2,1,0:T(8,128)(2,1)S(1)} fusion(bf16[16,132,512]{2,1,0:T(8,128)(2,1)S(1)} %bitcast.138, bf16[16,8,128]{2,1,0:T(8,128)(2,1)S(1)} %bitcast.144, s32[16,8,128]{2,1,0:T(8,128)S(1)} %convolution_convert_fusion.2, pred[16,8,128]{2,1,0:T(8,128)(4,1)S(1)} %bitcast.143), kind=kOutput, calls=%fused_computation.16 | convolution fusion | flops 608108544 | bytes 6930432 | tf_op jit(solution)/shard_map/blct,btd->blcd/dot_general | solution.py:60
  81.4 4.1 %constant_dynamic-slice_fusion = (bf16[4,1,8,36,512]{4,3,2,1,0:T(8,128)(2,1)}, bf16[4,1,8,36,512]{4,3,2,1,0:T(8,128)(2,1)}, bf16[4,1,8,36,512]{4,3,2,1,0:T(8,128...) fusion(bf16[4,4,8,36,512]{4,3,2,1,0:T(8,128)(2,1)S(1)} %bitcast, ...), kind=kLoop, calls=%fused_computation.92 | loop fusion | bytes 18874384 | tf_op jit(solution)/shard_map/jit(dynamic_index_in_dim)/dynamic_slice | solution.py:70
  85.5 5.0 %fusion.12 = f32[4,8,36]{2,0,1:T(4,128)S(1)} fusion(bf16[4,1,8,36,512]{4,3,2,1,0:T(8,128)(2,1)} %get-tuple-element.19, bf16[8,4,36,768]{3,1,2,0:T(4,128)(2,1)} %bitcast.140, bf16[8,768,512]{2,1,0:T(8,128)(2,1)} %param.9), kind=kOutput, calls=%fused_computation.25 | convolution fusion | flops 907737984 | bytes 9245184 | tf_op jit(solution)/shard_map/lscf,lfd->slcd/dot_general | solution.py:77
  90.5 0.6 broadcast_in_dim.109
  91.2 0.6 copy_dynamic-update-slice_fusion.3
  91.8 0.0 slice-start
  91.8 4.3 %fusion.11 = f32[4,8,36]{2,0,1:T(4,128)S(1)} fusion(bf16[4,1,8,36,512]{4,3,2,1,0:T(8,128)(2,1)S(1)} %copy-done.11, bf16[8,1,4,36,768]{4,0,3,2,1:T(8,128)(2,1)S(1)} %copy-done.4, bf16[8,768,512]{2,1,0:T(8,128)(2,1)} %param.9), kind=kOutput, calls=%fused_computation.23 | convolution fusion | flops 907737984 | bytes 9245184 | tf_op jit(solution)/shard_map/lscf,lfd->slcd/dot_general | solution.py:77
  96.1 0.6 copy_dynamic-update-slice_fusion.2
  96.8 4.6 %fusion.22 = bf16[8,512,768,1]{2,1,3,0:T(8,128)(2,1)} fusion(bf16[8,4,36,768]{3,1,2,0:T(4,128)(2,1)S(1)} %bitcast.141, bf16[4,1,8,36,512]{4,3,2,1,0:T(8,128)(2,1)S(1)} %copy-done.10), kind=kOutput, calls=%fused_computation.42 | convolution fusion | flops 905969664 | bytes 9240576 | tf_op jit(solution)/shard_map/lscf,slcd->lfd/dot_general | solution.py:72
  101.4 0.0 collective-permute-done.1
  101.4 2.3 %fusion.62 = (bf16[8,1,4,36,768]{4,0,3,2,1:T(8,128)(2,1)S(1)}, bf16[8,1,4,36,768]{4,0,3,2,1:T(8,128)(2,1)S(1)}) fusion(bf16[8,2,4,36,768]{4,0,3,2,1:T(8,128)(2,1)} %collective-permute-done.1), kind=kLoop, calls=%fused_computation.102 | loop fusion | bytes 7077888 | tf_op jit(solution)/shard_map/slice | solution.py:24
  103.8 0.0 copy-done.9
  103.8 1.6 %fusion.9 = f32[4,8,36]{2,0,1:T(4,128)S(1)} fusion(bf16[4,1,8,36,512]{4,3,2,1,0:T(8,128)(2,1)S(1)} %copy-done.9, bf16[8,768,512]{2,1,0:T(8,128)(2,1)S(1)} %bitcast.151, bf16[8,1,4,36,768]{4,0,3,2,1:T(8,128)(2,1)S(1)} %get-tuple-element.24), kind=kOutput, calls=%fused_computation.19 | convolution fusion | flops 907737984 | bytes 9245184 | tf_op jit(solution)/shard_map/lscf,lfd->slcd/dot_general | solution.py:77
  105.4 1.8 %fusion.10 = f32[4,8,36]{2,0,1:T(4,128)S(1)} fusion(bf16[4,1,8,36,512]{4,3,2,1,0:T(8,128)(2,1)S(1)} %copy-done.8, bf16[8,768,512]{2,1,0:T(8,128)(2,1)S(1)} %bitcast.151, bf16[8,1,4,36,768]{4,0,3,2,1:T(8,128)(2,1)S(1)} %get-tuple-element.25), kind=kOutput, calls=%fused_computation.21 | convolution fusion | flops 907737984 | bytes 9245184 | tf_op jit(solution)/shard_map/lscf,lfd->slcd/dot_general | solution.py:77
  107.1 0.6 copy_dynamic-update-slice_fusion.1
  107.8 0.6 copy_dynamic-update-slice_fusion
  108.4 1.6 %reshape.69 = f32[16,1,288]{2,1,0:T(1,128)} reshape(f32[16,8,36]{2,1,0:T(8,128)} %bitcast.44) | data formatting | bytes 36864
  109.9 4.1 %all-to-all-start.1 = ((f32[16,1,288]{2,1,0:T(1,128)}), f32[16,1,288]{2,1,0:T(1,128)}, u32[]{:S(2)}, u32[]{:S(2)}) async-start(f32[16,1,288]{2,1,0:T(1,128)} %reshape.69), calls=%async_computation.1 | async-start | bytes 49152 | tf_op jit(solution)/shard_map/all_to_all | solution.py:81
  114.1 3.4 %fusion.17 = bf16[8,768,512,1]{1,2,3,0:T(8,128)(2,1)S(1)} fusion(bf16[8,1,4,36,768]{4,0,3,2,1:T(8,128)(2,1)S(1)} %get-tuple-element.25, bf16[4,1,8,36,512]{4,3,2,1,0:T(8,128)(2,1)} %get-tuple-element.35), kind=kOutput, calls=%fused_computation.37 | convolution fusion | flops 905969664 | bytes 9240576 | tf_op jit(solution)/shard_map/lscf,slcd->lfd/dot_general | solution.py:72
  117.4 1.9 %fusion.18 = bf16[8,768,512,1]{1,2,3,0:T(8,128)(2,1)S(1)} fusion(bf16[8,1,4,36,768]{4,0,3,2,1:T(8,128)(2,1)S(1)} %get-tuple-element.24, bf16[4,1,8,36,512]{4,3,2,1,0:T(8,128)(2,1)S(1)} %copy-done), kind=kOutput, calls=%fused_computation.38 | convolution fusion | flops 905969664 | bytes 9240576 | tf_op jit(solution)/shard_map/lscf,slcd->lfd/dot_general | solution.py:72
  119.4 9.5 %fusion = f32[8,768,512]{1,2,0:T(8,128)} fusion(bf16[8,512,768,1]{2,1,3,0:T(8,128)(2,1)} %fusion.22, bf16[8,768,512,1]{1,2,3,0:T(8,128)(2,1)S(1)} %fusion.17, bf16[8,768,512,1]{1,2,3,0:T(8,128)(2,1)S(1)} %fusion.18, bf16[8,1,4,36,768]{4,0,3,2,1:T(8,128)(2,1)S(1)} %copy-done.5, bf16[4,1,8,36,512]{4,3,2,1,0:T(8,128)(2,1)} %get-tuple-element.37), kind=kOutput, calls=%fused_computation.3 | convolution fusion | flops 931135488 | bytes 34406400 | tf_op jit(solution)/shard_map/lscf,slcd->lfd/dot_general | solution.py:72
  128.9 12.6 %copy.190 = f32[8,768,512]{2,1,0:T(8,128)} copy(f32[8,768,512]{1,2,0:T(8,128)} %fusion) | data formatting | bytes 25165824
  141.5 0.0 all-to-all-done.1
  141.5 0.5 broadcast.17
  142.0 1.4 reduce
  143.4 0.1 reshape.70
  143.5 0.1 copy.188
  143.6 0.8 select_reduce_fusion
  144.5 0.6 select_reduce_fusion.1
  (31 shorter events, 0.1 us)
Async XLA Ops:
  7.2 66.9 %all-gather.3.cloned.1.call-start = ((), (), s32[]{:S(2)}) async-start(), calls=%async_computation.2 | async-start | bytes 2785280 | tf_op jit(solution)/shard_map/all_gather | solution.py:36
  10.9 14.0 %copy-start.6 = (bf16[8,1,4,36,768]{4,2,3,1,0:T(4,128)(2,1)S(1)}, bf16[8,1,4,36,768]{4,2,3,1,0:T(4,128)(2,1)}, u32[]{:S(2)}) copy-start(bf16[8,1,4,36,768]{4,2,3,1,0:T(4,128)(2,1)} %param.8) | copy-start | bytes 5308420
  24.8 1.0 copy-start.13
  25.4 40.5 %collective-permute-start = (bf16[8,1,4,36,768]{4,0,3,2,1:T(8,128)(2,1)S(1)}, bf16[8,1,4,36,768]{4,0,3,2,1:T(8,128)(2,1)S(1)}, u32[]{:S(2)}, u32[]{:S(2)}) collective-permute-start(bf16[8,1,4,36,768]{4,0,3,2,1:T(8,128)(2,1)S(1)} %copy.170), channel_id=1, source_target_pairs={{0,2},{1,3},{2,0},{3,1},{4,6},{5,7},{6,4},{7,5},{8,10},{9,11},{10,... | collective-permute-start | bytes 5308424 | tf_op jit(solution)/shard_map/ppermute | solution.py:20
  65.9 2.4 %copy-start.3 = (bf16[8,1,4,36,768]{4,0,3,2,1:T(8,128)(2,1)}, bf16[8,1,4,36,768]{4,0,3,2,1:T(8,128)(2,1)S(1)}, u32[]{:S(2)}) copy-start(bf16[8,1,4,36,768]{4,0,3,2,1:T(8,128)(2,1)S(1)} %collective-permute-done) | copy-start | bytes 5308420
  68.3 33.1 %collective-permute-start.1 = (bf16[8,2,4,36,768]{4,0,3,2,1:T(8,128)(2,1)}, bf16[8,2,4,36,768]{4,0,3,2,1:T(8,128)(2,1)}, u32[]{:S(2)}, u32[]{:S(2)}) collective-permute-start(bf16[8,2,4,36,768]{4,0,3,2,1:T(8,128)(2,1)} %pad_maximum_fusion), channel_id=1, source_target_pairs={{0,1},{1,0},{2,3},{3,2},{4,5},{5,4},{6,7},{7,6},{8,9},{9,8},{10,11... | collective-permute-start | bytes 10616840 | tf_op jit(solution)/shard_map/ppermute | solution.py:21
  75.4 2.9 %copy-start.1 = (bf16[16,132,1,512]{3,1,2,0:T(8,128)(2,1)S(1)}, bf16[16,132,1,512]{3,1,2,0:T(8,128)(2,1)}, u32[]{:S(2)}) copy-start(bf16[16,132,1,512]{3,1,2,0:T(8,128)(2,1)} %all-gather.3.cloned.1.call-done) | copy-start | bytes 6488068
  78.2 1.6 %copy-start.2 = (bf16[16,132,1,512]{3,1,2,0:T(8,128)(2,1)S(1)}, bf16[16,132,1,512]{3,1,2,0:T(8,128)(2,1)}, u32[]{:S(2)}) copy-start(bf16[16,132,1,512]{3,1,2,0:T(8,128)(2,1)} %all-gather.3.cloned.1.call-done) | copy-start | bytes 6488068
  85.5 6.3 %copy-start.4 = (bf16[8,1,4,36,768]{4,0,3,2,1:T(8,128)(2,1)S(1)}, bf16[8,1,4,36,768]{4,0,3,2,1:T(8,128)(2,1)}, u32[]{:S(2)}) copy-start(bf16[8,1,4,36,768]{4,0,3,2,1:T(8,128)(2,1)} %copy-done.3) | copy-start | bytes 5308420
  85.5 6.3 %copy-start.11 = (bf16[4,1,8,36,512]{4,3,2,1,0:T(8,128)(2,1)S(1)}, bf16[4,1,8,36,512]{4,3,2,1,0:T(8,128)(2,1)}, u32[]{:S(2)}) copy-start(bf16[4,1,8,36,512]{4,3,2,1,0:T(8,128)(2,1)} %get-tuple-element.18) | copy-start | bytes 3538948
  91.8 5.0 %copy-start.7 = (bf16[8,1,4,36,768]{4,2,3,1,0:T(4,128)(2,1)S(1)}, bf16[8,1,4,36,768]{4,2,3,1,0:T(4,128)(2,1)}, u32[]{:S(2)}) copy-start(bf16[8,1,4,36,768]{4,2,3,1,0:T(4,128)(2,1)} %param.8) | copy-start | bytes 5308420
  91.8 5.0 %copy-start.10 = (bf16[4,1,8,36,512]{4,3,2,1,0:T(8,128)(2,1)S(1)}, bf16[4,1,8,36,512]{4,3,2,1,0:T(8,128)(2,1)}, u32[]{:S(2)}) copy-start(bf16[4,1,8,36,512]{4,3,2,1,0:T(8,128)(2,1)} %get-tuple-element.34) | copy-start | bytes 3538948
  91.8 12.0 %slice-start = ((s8[6291456]{0:T(1024)(128)(4,1)}), s8[2097152]{0:T(1024)(128)(4,1)S(1)}, s32[]{:S(2)}) async-start(s8[6291456]{0:T(1024)(128)(4,1)} %bitcast.150), calls=%async_computation.3 | async-start | bytes 4194304
  96.8 7.0 %slice-start.1 = ((s8[6291456]{0:T(1024)(128)(4,1)}), s8[4194304]{0:T(1024)(128)(4,1)S(1)}, s32[]{:S(2)}) async-start(s8[6291456]{0:T(1024)(128)(4,1)} %bitcast.150), calls=%async_computation.4 | async-start | bytes 8388608
  101.4 2.4 %copy-start.9 = (bf16[4,1,8,36,512]{4,3,2,1,0:T(8,128)(2,1)S(1)}, bf16[4,1,8,36,512]{4,3,2,1,0:T(8,128)(2,1)}, u32[]{:S(2)}) copy-start(bf16[4,1,8,36,512]{4,3,2,1,0:T(8,128)(2,1)} %get-tuple-element.16) | copy-start | bytes 3538948
  103.8 1.6 %copy-start.8 = (bf16[4,1,8,36,512]{4,3,2,1,0:T(8,128)(2,1)S(1)}, bf16[4,1,8,36,512]{4,3,2,1,0:T(8,128)(2,1)}, u32[]{:S(2)}) copy-start(bf16[4,1,8,36,512]{4,3,2,1,0:T(8,128)(2,1)} %get-tuple-element.17) | copy-start | bytes 3538948
  109.9 31.6 %all-to-all-start.1 = ((f32[16,1,288]{2,1,0:T(1,128)}), f32[16,1,288]{2,1,0:T(1,128)}, u32[]{:S(2)}, u32[]{:S(2)}) async-start(f32[16,1,288]{2,1,0:T(1,128)} %reshape.69), calls=%async_computation.1 | async-start | bytes 49152 | tf_op jit(solution)/shard_map/all_to_all | solution.py:81
  114.0 3.4 %copy-start = (bf16[4,1,8,36,512]{4,3,2,1,0:T(8,128)(2,1)S(1)}, bf16[4,1,8,36,512]{4,3,2,1,0:T(8,128)(2,1)}, u32[]{:S(2)}) copy-start(bf16[4,1,8,36,512]{4,3,2,1,0:T(8,128)(2,1)} %get-tuple-element.36) | copy-start | bytes 3538948
  117.4 2.0 %copy-start.5 = (bf16[8,1,4,36,768]{4,0,3,2,1:T(8,128)(2,1)S(1)}, bf16[8,1,4,36,768]{4,0,3,2,1:T(8,128)(2,1)}, u32[]{:S(2)}) copy-start(bf16[8,1,4,36,768]{4,0,3,2,1:T(8,128)(2,1)} %copy-done.3) | copy-start | bytes 5308420
  128.9 14.8 %copy-start.12 = (pred[128,8,32]{0,2,1:T(8,128)(4,1)S(1)}, pred[128,8,32]{0,2,1:T(8,128)(4,1)}, u32[]{:S(2)}) copy-start(pred[128,8,32]{0,2,1:T(8,128)(4,1)} %get-tuple-element.33) | copy-start | bytes 98308
Sparse Core Ops, SparseCore 0:
  24.9 49.0 all-gather.2
